TPU v7x, 256 devices: a whole 4x4x8 slice. The times are simulated.
256 devices in a mesh: dp: 16 (over y, x), section: 2 (over core), tensor: 8 (over z).
Axes of the slice: x: 4, y: 4, z: 8, core: 2. Of those that a mesh axis runs over, the one named last changes fastest.
Arguments:
- tokens: bfloat16 [2048, 16384], P('dp'), may hold values from -9 to 9
- order: int32 [2048], replicated, may hold values from 0 to 2047, as said below
- segments: int32 [2048], replicated, may hold values from 0 to 1, as said below
- gain: float32 [2, 16384], P('section', 'dp'), may hold values from 0.1 to 1.9
- w_query: bfloat16 [2, 16384, 8192], P('section', 'dp', 'tensor'), may hold values from -0.046875 to 0.046875
- key_value_weight: bfloat16 [2, 16384, 8, 256], P('section', 'dp', 'tensor'), may hold values from -0.046875 to 0.046875
- w_out: bfloat16 [2, 8192, 16384], P('section', 'tensor', 'dp'), may hold values from -0.0625 to 0.0625
Outputs:
- layer_out: bfloat16 [2048, 16384], P('section', 'dp')
Inputs may be any that keep to these rules, and one draw needn't show every extreme that they name: A permutation that moves whole sentences: the rows of one sentence (a run of equal segments within a block of 32 rows) come from consecutive entry rows in order. `segments`: within each block of 32 rows the sentence numbers do not fall and each of 0 to 1 appears.
All inputs are finite; a program needn't handle non-finite values.
Results may differ from a plain program's by a relative error of at most 0.022.
Values may be sent and summed in bfloat16 or wider, within the bound.
No kernel may reach another device: no remote copies, remote signals or barrier semaphores. Data moves between devices by JAX's collectives and lax.ppermute only.
A program may use at most 64 MiB of HBM per device.

v0:
```python
import math
import jax
import jax.numpy as jnp
from jax import lax
from jax.experimental.layout import Layout, with_layout_constraint
from jax.sharding import PartitionSpec as P

MODEL_WIDTH = 16384
KEYVALUE_HEADS = 8
QUERY_HEADS = 64
MICRO_TOKENS = 32
HEAD_WIDTH = 128
SPARE_COLUMNS = 128
M = 4
norm_epsilon = 1e-05


def causal_block_attend(query_rows, key_value_rows, allowed, query_group_width):
    block_count, row_count = allowed.shape[:2]
    kv_heads = key_value_rows.shape[1]
    head_size = key_value_rows.shape[2] // 2
    query_head_rows = query_rows.reshape(
        block_count, row_count, kv_heads, query_group_width, head_size
    )
    key_value_blocks = key_value_rows.reshape(block_count, row_count, kv_heads, 2 * head_size)
    key_heads = key_value_blocks[..., :head_size]
    value_heads = key_value_blocks[..., head_size:]
    scores = jnp.einsum(
        "bqkgd,bskd->bkgqs", query_head_rows, key_heads, preferred_element_type=jnp.float32
    ) / math.sqrt(head_size)
    raw_weights = jnp.where(allowed[:, None, None], jnp.exp(scores), 0.0)
    totals = jnp.sum(raw_weights, axis=-1, keepdims=True)
    probs = (raw_weights / totals).astype(jnp.bfloat16)
    attended_rows = jnp.einsum(
        "bkgqs,bskd->bqkgd", probs, value_heads, preferred_element_type=jnp.float32
    )
    return attended_rows.astype(jnp.bfloat16).reshape(
        block_count * row_count, kv_heads * query_group_width * head_size
    )


def block_mask(sentence_segment_rows):
    row_count = sentence_segment_rows.shape[1]
    position = jnp.arange(row_count)
    return (sentence_segment_rows[:, :, None] == sentence_segment_rows[:, None, :]) & (
        position[None, :] <= position[:, None]
    )[None]


def gathered_over(block, axis):
    count = lax.axis_size(axis)
    spread = jnp.broadcast_to(block[None], (count,) + block.shape)
    return lax.all_to_all(spread, axis, 0, 0, tiled=False).reshape(
        (count * block.shape[0],) + block.shape[1:]
    )


def section_layer(hidden, own_allowed, gain_row, joined_weight, out_weight):
    row_count = hidden.shape[0]
    group_count = lax.axis_size("dp")
    own_rows = row_count // group_count
    widened = hidden.astype(jnp.float32)
    normed_rows = (widened * gain_row[None, :]).astype(jnp.bfloat16)
    joined_terms = jnp.dot(normed_rows, joined_weight, preferred_element_type=jnp.float32)
    query_width = out_weight.shape[0]
    keyval_width = joined_terms.shape[1] - query_width - SPARE_COLUMNS
    square_terms = jnp.sum(widened * widened, axis=1, keepdims=True)
    square_high = lax.reduce_precision(square_terms, exponent_bits=8, mantissa_bits=7)
    square_low = square_terms - square_high
    column = lax.broadcasted_iota(jnp.int32, joined_terms.shape, 1)
    square_column = query_width + keyval_width
    payload = jnp.where(
        column == square_column,
        square_high,
        jnp.where(column == square_column + 1, square_low, joined_terms),
    ).astype(jnp.bfloat16)
    arrived = lax.all_to_all(
        payload.reshape(group_count, own_rows, payload.shape[1]), "dp", 0, 0, tiled=False
    )
    summed = jnp.sum(arrived.astype(jnp.float32), axis=0)
    own_squares = summed[:, query_width + keyval_width] + summed[:, query_width + keyval_width + 1]
    root_mean_square = jnp.sqrt(own_squares / MODEL_WIDTH + norm_epsilon)
    scaled_sums = summed[:, : query_width + keyval_width] / root_mean_square[:, None]
    query_rows = scaled_sums[:, :query_width].astype(jnp.bfloat16)
    key_value_rows = (
        scaled_sums[:, query_width:].astype(jnp.bfloat16).reshape(own_rows, -1, 2 * HEAD_WIDTH)
    )
    attended_rows = causal_block_attend(
        query_rows, key_value_rows, own_allowed, QUERY_HEADS // KEYVALUE_HEADS
    )
    head_terms = jnp.dot(
        gathered_over(attended_rows, "dp"), out_weight, preferred_element_type=jnp.float32
    )
    head_total = lax.psum(head_terms.astype(jnp.bfloat16), "tensor").astype(jnp.float32)
    return (widened + head_total).astype(jnp.bfloat16)


def on_device(tokens, order, segments, gain, w_query, key_value_weight, w_out):
    section_count = lax.axis_size("section")
    section_index = lax.axis_index("section")
    group_count = lax.axis_size("dp")
    slice_width = w_query.shape[1]
    joined = jnp.concatenate(
        [
            w_query[0],
            key_value_weight[0].reshape(slice_width, -1),
            jnp.zeros((slice_width, SPARE_COLUMNS), w_query.dtype),
        ],
        axis=1,
    )
    own = (gain[0], joined, w_out[0])
    swap = [(i, (i + 1) % section_count) for i in range(section_count)]
    other = lax.ppermute(own, "section", swap)
    entry_rows, model_width = tokens.shape
    part_rows = entry_rows // section_count
    my_rows = lax.dynamic_slice_in_dim(tokens, section_index * part_rows, part_rows)
    got = lax.all_to_all(
        my_rows.reshape(part_rows, group_count, model_width // group_count), "dp", 1, 0, tiled=True
    ).reshape(group_count * part_rows, -1)
    received = lax.ppermute(got, "section", swap)
    rows_here = group_count * entry_rows // section_count
    own_blocks = rows_here // (group_count * MICRO_TOKENS)
    own_segments = lax.dynamic_slice_in_dim(
        segments,
        section_index * rows_here + lax.axis_index("dp") * own_blocks * MICRO_TOKENS,
        own_blocks * MICRO_TOKENS,
    ).reshape(own_blocks, MICRO_TOKENS)
    other, received, own_allowed = lax.optimization_barrier(
        (other, received, block_mask(own_segments))
    )
    my_order = lax.dynamic_slice_in_dim(order, section_index * rows_here, rows_here)
    source_group = my_order // entry_rows
    within = my_order % entry_rows
    from_other = within // part_rows != section_index
    block_index = source_group * part_rows + within % part_rows
    hits = lax.broadcasted_iota(jnp.int32, (rows_here, got.shape[0]), 1) == block_index[:, None]
    picked_here = (hits & ~from_other[:, None]).astype(got.dtype)
    picked_there = (hits & from_other[:, None]).astype(got.dtype)
    hidden = (
        jnp.dot(picked_here, got, preferred_element_type=jnp.float32)
        + jnp.dot(picked_there, received, preferred_element_type=jnp.float32)
    ).astype(got.dtype)
    hidden = with_layout_constraint(hidden, Layout(major_to_minor=(0, 1)))
    for layer_index in range(section_count):
        params = jax.tree.map(
            lambda mine, theirs: jnp.where(section_index == layer_index, mine, theirs), own, other
        )
        hidden = section_layer(hidden, own_allowed, *params)
    return hidden


def solution(mesh):
    placed = (
        P("dp", None),
        P(),
        P(),
        P("section", "dp"),
        P("section", "dp", "tensor"),
        P("section", "dp", "tensor", None),
        P("section", "tensor", "dp"),
    )
    return jax.shard_map(
        on_device, mesh=mesh, in_specs=placed, out_specs=P("section", "dp"), check_vma=False
    )
```

profile of v0, /device:TPU:2, one launch (start us, length us, event | category | flops | bytes accessed | tf_op | source)
XLA Modules:
  0.0 392.8 jit_solution(6139880613853147727)
XLA Ops:
  6.5 1.7 constant_dynamic-slice_fusion
  8.3 1.6 copy.54
  9.8 0.0 copy-start.1
  9.8 0.0 copy-start.4
  9.8 7.7 %all-to-all-start = ((bf16[64,16,1024]{2,0,1:T(8,128)(2,1)}), bf16[64,16,1024]{2,0,1:T(8,128)(2,1)}, u32[]{:S(2)}, u32[]{:S(2)}) async-start(bf16[64,16,1024]{2,0,1:T(8,128)(2,1)} %bitcast.102), calls=%async_computation | async-start | bytes 4194304 | tf_op jit(solution)/shard_map/all_to_all | solution.py:117
  17.6 0.0 copy-start.6
  17.6 0.0 copy-start.5
  17.6 0.0 all-reduce.3.cloned.1.call-start
  17.7 0.0 copy-done.1
  17.7 0.0 copy-done.4
  17.7 2.2 maximum_maximum_fusion
  19.9 0.0 collective-permute-start.1
  19.9 0.5 collective-permute-start.2
  20.4 24.4 %all-to-all-done = bf16[64,16,1024]{2,0,1:T(8,128)(2,1)} async-done(((bf16[64,16,1024]{2,0,1:T(8,128)(2,1)}), bf16[64,16,1024]{2,0,1:T(8,128)(2,1)}, u32[]{:S(2)}, u32[]{:S(2)}) %all-to-all-start) | async-done | bytes 2097184 | tf_op jit(solution)/shard_map/all_to_all | solution.py:117
  44.8 0.0 collective-permute-start.3
  44.8 0.0 copy-done.6
  44.8 0.5 collective-permute-start
  45.3 0.8 dynamic_slice.11
  46.1 0.1 eq.52
  46.2 0.0 copy-done.5
  46.2 0.1 compare_and_fusion
  46.3 4.0 %fusion.8 = f32[1024,1024]{1,0:T(8,128)S(1)} fusion(bf16[1024,1024]{1,0:T(8,128)(2,1)} %bitcast.2, s32[1024]{0:T(1024)S(1)} %fusion.61, pred[1024]{0:T(1024)(128)(4,1)S(1)} %get-tuple-element.15), kind=kOutput, calls=%fused_computation.20 | convolution fusion | flops 2149580800 | bytes 6296576 | tf_op jit(solution)/shard_map/dot_general | solution.py:140
  50.3 0.0 collective-permute-done
  50.3 0.0 collective-permute-done.2
  50.3 0.0 collective-permute-done.1
  50.3 0.0 collective-permute-done.3
  50.3 0.0 copy-start.2
  50.4 4.9 %fusion = (f32[1024]{0:T(1024)S(1)}, bf16[1024,1024]{1,0:T(8,128)(2,1)S(1)}) fusion(f32[1024,1024]{1,0:T(8,128)S(1)} %fusion.8, bf16[1024,1024]{1,0:T(8,128)(2,1)} %collective-permute-done.3, s32[1024]{0:T(1024)S(1)} %fusion.61, pred[1024]{0:T(1024)(128)(4,1)S(1)} %get-tuple-element.16), kind=kOutput, calls=%fused_computation.10 | convolution fusion | flops 2154822656 | bytes 8397824 | tf_op jit(solution)/shard_map/dot_general | solution.py:141
  55.3 0.0 copy-done.2
  55.3 3.6 select_convert_fusion.1
  58.9 44.4 %all_to_all.35 = bf16[16,64,1408]{2,1,0:T(8,128)(2,1)S(1)} all-to-all(bf16[16,64,1408]{2,1,0:T(8,128)(2,1)S(1)} %bitcast.107), channel_id=1, replica_groups=mesh['dp'=16,'section'=2,'tensor'=8] {'dp'}, dimensions={0} | all-to-all | bytes 5767168 | tf_op jit(solution)/shard_map/all_to_all | solution.py:77
  103.3 0.4 convert_reduce_fusion.1
  103.6 0.2 fusion.59
  103.8 0.1 fusion.47
  104.0 0.3 fusion.73
  104.3 0.2 fusion.44
  104.6 0.1 copy.28
  104.7 0.3 broadcast_in_dim.78
  104.9 32.2 %all_to_all.36 = bf16[16,64,1024]{2,1,0:T(8,128)(2,1)S(1)} all-to-all(bf16[16,64,1024]{2,1,0:T(8,128)(2,1)S(1)} %broadcast_in_dim.78), channel_id=1, replica_groups=mesh['dp'=16,'section'=2,'tensor'=8] {'dp'}, dimensions={0} | all-to-all | bytes 4194304 | tf_op jit(solution)/shard_map/all_to_all | solution.py:53
  137.1 5.3 %fusion.30 = bf16[1024,1024]{1,0:T(8,128)(2,1)} fusion(bf16[1024,1024]{1,0:T(8,128)(2,1)S(1)} %bitcast.112, bf16[1024,1024]{1,0:T(8,128)(2,1)} %collective-permute-done.2, pred[]{:T(512)S(6)} %eq.58, bf16[1,1024,1024]{2,1,0:T(8,128)(2,1)} %param.13), kind=kOutput, calls=%fused_computation.40 | convolution fusion | flops 2149580800 | bytes 8388609 | tf_op jit(solution)/shard_map/dot_general | solution.py:91
  142.4 0.0 all-reduce.3.cloned.1.call-update
  142.4 0.0 all-reduce.5.cloned.1.call-start
  142.4 82.2 %all-reduce.3.cloned.1.call-done = bf16[1024,1024]{1,0:T(8,128)(2,1)} async-done(((bf16[1024,1024]{1,0:T(8,128)(2,1)}), bf16[1024,1024]{1,0:T(8,128)(2,1)}) %all-reduce.3.cloned.1.call-update) | async-done | bytes 2097168 | tf_op jit(solution)/shard_map/psum | solution.py:94
  224.6 0.0 copy-start
  224.6 0.0 copy-start.3
  224.6 2.5 fusion.3
  227.1 0.0 copy-done
  227.1 0.3 copy-done.3
  227.5 5.4 %select_convert_fusion = bf16[1024,1408]{1,0:T(8,128)(2,1)S(1)} fusion(bf16[1024,1408]{1,0:T(8,128)(2,1)} %collective-permute-done.1, bf16[1024]{0:T(1024)(128)(2,1)S(1)} %get-tuple-element.20, bf16[1024]{0:T(1024)(128)(2,1)S(1)} %get-tuple-element.19, pred[]{:T(512)S(6)} %eq.59, pred[1408]{0:T(1024)(128)(4,1)S(1)} %get-tuple-element.29, ...), kind=kOutput, calls=%fused_computation.7 | convolution fusion | flops 2973106176 | bytes 12596737 | tf_op jit(solution)/shard_map/dot_general | solution.py:64
  232.9 37.0 %all_to_all.37 = bf16[16,64,1408]{2,1,0:T(8,128)(2,1)S(1)} all-to-all(bf16[16,64,1408]{2,1,0:T(8,128)(2,1)S(1)} %bitcast.106), channel_id=1, replica_groups=mesh['dp'=16,'section'=2,'tensor'=8] {'dp'}, dimensions={0} | all-to-all | bytes 5767168 | tf_op jit(solution)/shard_map/all_to_all | solution.py:77
  269.8 0.4 convert_reduce_fusion
  270.2 0.2 fusion.55
  270.4 0.1 fusion.46
  270.6 0.3 fusion.74
  270.9 0.2 fusion.45
  271.2 0.1 copy.31
  271.2 0.3 broadcast_in_dim.82
  271.5 25.5 %all_to_all.38 = bf16[16,64,1024]{2,1,0:T(8,128)(2,1)S(1)} all-to-all(bf16[16,64,1024]{2,1,0:T(8,128)(2,1)S(1)} %broadcast_in_dim.82), channel_id=1, replica_groups=mesh['dp'=16,'section'=2,'tensor'=8] {'dp'}, dimensions={0} | all-to-all | bytes 4194304 | tf_op jit(solution)/shard_map/all_to_all | solution.py:53
  297.0 5.9 %fusion.33 = bf16[1024,1024]{1,0:T(8,128)(2,1)} fusion(bf16[1024,1024]{1,0:T(8,128)(2,1)S(1)} %bitcast.111, bf16[1024,1024]{1,0:T(8,128)(2,1)} %collective-permute-done.2, pred[]{:T(512)S(6)} %eq.59, bf16[1,1024,1024]{2,1,0:T(8,128)(2,1)} %param.13), kind=kOutput, calls=%fused_computation.41 | convolution fusion | flops 2149580800 | bytes 8388609 | tf_op jit(solution)/shard_map/dot_general | solution.py:91
  302.9 0.0 all-reduce.5.cloned.1.call-update
  302.9 78.0 %all-reduce.5.cloned.1.call-done = bf16[1024,1024]{1,0:T(8,128)(2,1)} async-done(((bf16[1024,1024]{1,0:T(8,128)(2,1)}), bf16[1024,1024]{1,0:T(8,128)(2,1)}) %all-reduce.5.cloned.1.call-update) | async-done | bytes 2097168 | tf_op jit(solution)/shard_map/psum | solution.py:94
  380.9 5.0 %fusion.5 = bf16[1024,1024]{1,0:T(8,128)(2,1)} fusion(bf16[1024,1024]{1,0:T(8,128)(2,1)} %all-reduce.5.cloned.1.call-done, bf16[1024,1024]{1,0:T(8,128)(2,1)} %all-reduce.3.cloned.1.call-done, bf16[1024,1024]{1,0:T(8,128)(2,1)S(1)} %get-tuple-element.24), kind=kLoop, calls=%fused_computation.15 | loop fusion | flops 8388608 | bytes 8388608 | tf_op jit(solution)/shard_map/convert_element_type | solution.py:95
  (17 shorter events, 0.2 us)
Async XLA Ops:
  9.8 7.8 %copy-start.1 = (bf16[1,1024,1024]{2,1,0:T(8,128)(2,1)S(1)}, bf16[1,1024,1024]{2,1,0:T(8,128)(2,1)}, u32[]{:S(2)}) copy-start(bf16[1,1024,1024]{2,1,0:T(8,128)(2,1)} %param.11) | copy-start | bytes 6291460
  9.8 7.8 %copy-start.4 = (bf16[1,1024,1,256]{3,1,2,0:T(8,128)(2,1)S(1)}, bf16[1,1024,1,256]{3,1,2,0:T(8,128)(2,1)}, u32[]{:S(2)}) copy-start(bf16[1,1024,1,256]{3,1,2,0:T(8,128)(2,1)} %param.12) | copy-start | bytes 1572868
  9.8 35.0 %all-to-all-start = ((bf16[64,16,1024]{2,0,1:T(8,128)(2,1)}), bf16[64,16,1024]{2,0,1:T(8,128)(2,1)}, u32[]{:S(2)}, u32[]{:S(2)}) async-start(bf16[64,16,1024]{2,0,1:T(8,128)(2,1)} %bitcast.102), calls=%async_computation | async-start | bytes 4194304 | tf_op jit(solution)/shard_map/all_to_all | solution.py:117
  17.6 27.2 %copy-start.6 = (f32[1,1024]{1,0:T(1,128)S(1)}, f32[1,1024]{1,0:T(1,128)}, u32[]{:S(2)}) copy-start(f32[1,1024]{1,0:T(1,128)} %param.10) | copy-start | bytes 12292
  17.6 28.6 %copy-start.5 = (s32[2048]{0:T(1024)S(1)}, s32[2048]{0:T(1024)}, u32[]{:S(2)}) copy-start(s32[2048]{0:T(1024)} %param.8) | copy-start | bytes 24580
  17.6 207.0 %all-reduce.3.cloned.1.call-start = ((), (), s32[]{:S(2)}) async-start(), calls=%async_computation.5 | async-start | bytes 4194304 | tf_op jit(solution)/shard_map/psum | solution.py:94
  19.9 30.4 %collective-permute-start.1 = (bf16[1024,1408]{1,0:T(8,128)(2,1)}, bf16[1024,1408]{1,0:T(8,128)(2,1)}, u32[]{:S(2)}, u32[]{:S(2)}) collective-permute-start(bf16[1024,1408]{1,0:T(8,128)(2,1)} %maximum_maximum_fusion), channel_id=1, source_target_pairs={{0,8},{8,0},{1,9},{9,1},{2,10},{10,2},{3,11},{11,3},{4,12},{12,4},... | collective-permute-start | bytes 8650760 | tf_op jit(solution)/shard_map/ppermute | solution.py:113
  19.9 30.4 %collective-permute-start.2 = (bf16[1024,1024]{1,0:T(8,128)(2,1)}, bf16[1024,1024]{1,0:T(8,128)(2,1)}, u32[]{:S(2)}, u32[]{:S(2)}) collective-permute-start(bf16[1024,1024]{1,0:T(8,128)(2,1)} %bitcast.6), channel_id=1, source_target_pairs={{0,8},{8,0},{1,9},{9,1},{2,10},{10,2},{3,11},{11,3},{4,12},{12,4},... | collective-permute-start | bytes 6291464 | tf_op jit(solution)/shard_map/ppermute | solution.py:113
  44.8 5.5 %collective-permute-start.3 = (bf16[1024,1024]{1,0:T(8,128)(2,1)}, bf16[1024,1024]{1,0:T(8,128)(2,1)}, u32[]{:S(2)}, u32[]{:S(2)}) collective-permute-start(bf16[1024,1024]{1,0:T(8,128)(2,1)} %bitcast.2), channel_id=1, source_target_pairs={{0,8},{8,0},{1,9},{9,1},{2,10},{10,2},{3,11},{11,3},{4,12},{12,4},... | collective-permute-start | bytes 6291464 | tf_op jit(solution)/shard_map/ppermute | solution.py:120
  44.8 5.5 %collective-permute-start = (f32[1024]{0:T(1024)S(1)}, f32[1024]{0:T(1024)S(1)}, u32[]{:S(2)}, u32[]{:S(2)}) collective-permute-start(f32[1024]{0:T(1024)S(1)} %bitcast.126), channel_id=1, source_target_pairs={{0,8},{8,0},{1,9},{9,1},{2,10},{10,2},{3,11},{11,3},{4,12},{12,4},... | collective-permute-start | bytes 12296 | tf_op jit(solution)/shard_map/ppermute | solution.py:113
  50.3 4.9 %copy-start.2 = (bf16[1,1024,1024]{2,1,0:T(8,128)(2,1)S(1)}, bf16[1,1024,1024]{2,1,0:T(8,128)(2,1)}, u32[]{:S(2)}) copy-start(bf16[1,1024,1024]{2,1,0:T(8,128)(2,1)} %param.11) | copy-start | bytes 6291460
  142.4 238.5 %all-reduce.5.cloned.1.call-start = ((), (), s32[]{:S(2)}) async-start(), calls=%async_computation.6 | async-start | bytes 4194304 | tf_op jit(solution)/shard_map/psum | solution.py:94
  224.6 2.5 copy-start
  224.6 2.9 copy-start.3
Sparse Core Ops, SparseCore 0:
  142.5 82.0 all-reduce.2
  303.1 77.8 all-reduce.4
where the time goes:
time: 393 us
  waiting for transfers between devices  185 us (47%)
  blocking collectives  139 us (35%)
  matrix products  30.1 us (8%)
  between operations  13.7 us (3%)
  other arithmetic  11.2 us (3%)
  starting transfers between devices  8.84 us (2%)
  local copies, waits for them, and re-layouts  5.23 us (1%)
    psum x2, waiting for transfers between devices, section_layer(): lax.psum(head_terms.astype(jnp.bfloat16), 'tensor').astype(jnp.float32)  160 us
    all_to_all x2, blocking collectives, section_layer(): lax.all_to_all(payload.reshape(group_count, own_rows, payload.shape[1]),...  81.4 us
    all_to_all x2, blocking collectives, gathered_over(): lax.all_to_all(spread, axis, 0, 0, tiled=False)  57.7 us
    all_to_all x1, waiting for transfers between devices, on_device(): lax.all_to_all(my_rows.reshape(part_rows, group_count, model_width // gro...  24.4 us
    dot_general x2, matrix products, section_layer(): jnp.dot(gathered_over(attended_rows, 'dp'), out_weight, preferred_element...  11.2 us
    dot_general x2, matrix products, section_layer(): jnp.dot(normed_rows, joined_weight, preferred_element_type=jnp.float32)  8.97 us
  transfers between devices with their start and end apart: 7, of which 3 were waited for; matrix products, arithmetic and copies ran while one was open for 2% of the time, Pallas kernels for 0%

commit v1 on v0

--- a/solution.py
+++ b/solution.py
@@ -91,7 +91,9 @@
     head_terms = jnp.dot(
         gathered_over(attended_rows, "dp"), out_weight, preferred_element_type=jnp.float32
     )
-    head_total = lax.psum(head_terms.astype(jnp.bfloat16), "tensor").astype(jnp.float32)
+    head_total = jnp.sum(lax.all_gather(head_terms.astype(jnp.bfloat16), "tensor"), axis=0).astype(
+        jnp.float32
+    )
     return (widened + head_total).astype(jnp.bfloat16)
 
 

time: 393 us -> 602 us (1.53)
  waiting for transfers between devices: 185 us -> 366 us
  other arithmetic: 11.2 us -> 31.5 us
  blocking collectives: 139 us -> 146 us
    all_gather x0 -> x2, waiting for transfers between devices: none -> 341 us  [section_layer(): lax.all_gather(head_terms.astype(jnp.bfloat16), 'tensor')]
    psum x2 -> x0, waiting for transfers between devices: 160 us -> none  [section_layer(): lax.psum(head_terms.astype(jnp.bfloat16), 'tensor').astype(jnp.float32)]
    reduce_sum x0 -> x2, other arithmetic: none -> 20.2 us  [section_layer(): jnp.sum(lax.all_gather(head_terms.astype(jnp.bfloat16), 'tensor'), axis=0)]
  transfers between devices with their start and end apart: 7 -> 7, of which waited for: 3 -> 3; matrix products, arithmetic and copies ran while one was open for 2% -> 1% of each run, Pallas kernels for 0% -> 0%
where the time goes in v1:
time: 602 us; the launch traced here: 601 us
  waiting for transfers between devices  366 us (61%)
  blocking collectives  146 us (24%)
  other arithmetic  31.5 us (5%)
  matrix products  30.1 us (5%)
  between operations  13.8 us (2%)
  starting transfers between devices  8.79 us (1%)
    all_gather x2, waiting for transfers between devices, section_layer(): lax.all_gather(head_terms.astype(jnp.bfloat16), 'tensor')  341 us
    all_to_all x2, blocking collectives, section_layer(): lax.all_to_all(payload.reshape(group_count, own_rows, payload.shape[1]),...  84.3 us
    all_to_all x2, blocking collectives, gathered_over(): lax.all_to_all(spread, axis, 0, 0, tiled=False)  61.4 us
    all_to_all x1, waiting for transfers between devices, on_device(): lax.all_to_all(my_rows.reshape(part_rows, group_count, model_width // gro...  24.3 us
    reduce_sum x2, other arithmetic, section_layer(): jnp.sum(lax.all_gather(head_terms.astype(jnp.bfloat16), 'tensor'), axis=0)  20.2 us
  transfers between devices with their start and end apart: 7, of which 3 were waited for; matrix products, arithmetic and copies ran while one was open for 1% of the time, Pallas kernels for 0%

profile of v1, /device:TPU:2, one launch (start us, length us, event | category | flops | bytes accessed | tf_op | source)
XLA Modules:
  0.0 600.8 jit_solution(11916533676684049530)
XLA Ops:
  6.5 1.7 constant_dynamic-slice_fusion
  8.3 1.5 copy.54
  9.8 0.0 copy-start.4
  9.8 7.6 %all-to-all-start = ((bf16[64,16,1024]{2,0,1:T(8,128)(2,1)}), bf16[64,16,1024]{2,0,1:T(8,128)(2,1)}, u32[]{:S(2)}, u32[]{:S(2)}) async-start(bf16[64,16,1024]{2,0,1:T(8,128)(2,1)} %bitcast.104), calls=%async_computation | async-start | bytes 4194304 | tf_op jit(solution)/shard_map/all_to_all | solution.py:119
  17.4 0.0 copy-start.6
  17.4 0.0 copy-start.5
  17.4 0.0 all-gather.5.cloned.1.call-start
  17.5 0.0 copy-done.4
  17.5 2.2 maximum_maximum_fusion
  19.7 0.1 collective-permute-start.1
  19.8 0.5 collective-permute-start.2
  20.3 24.3 %all-to-all-done = bf16[64,16,1024]{2,0,1:T(8,128)(2,1)} async-done(((bf16[64,16,1024]{2,0,1:T(8,128)(2,1)}), bf16[64,16,1024]{2,0,1:T(8,128)(2,1)}, u32[]{:S(2)}, u32[]{:S(2)}) %all-to-all-start) | async-done | bytes 2097184 | tf_op jit(solution)/shard_map/all_to_all | solution.py:119
  44.6 0.0 collective-permute-start.3
  44.6 0.0 copy-done.6
  44.6 0.5 collective-permute-start
  45.1 0.8 dynamic_slice.11
  45.9 0.1 eq.52
  46.0 0.0 copy-done.5
  46.0 0.1 compare_and_fusion
  46.1 4.0 fusion.8
  50.1 0.0 collective-permute-done
  50.1 0.0 collective-permute-done.2
  50.1 0.0 collective-permute-done.1
  50.1 0.0 collective-permute-done.3
  50.1 0.0 copy-start.2
  50.2 4.9 fusion
  55.0 0.0 copy-start
  55.1 0.0 copy-done.2
  55.1 3.5 select_convert_fusion.1
  58.6 0.0 copy-done
  58.6 43.6 %all_to_all.35 = bf16[16,64,1408]{2,1,0:T(8,128)(2,1)S(1)} all-to-all(bf16[16,64,1408]{2,1,0:T(8,128)(2,1)S(1)} %bitcast.111), channel_id=1, replica_groups=mesh['dp'=16,'section'=2,'tensor'=8] {'dp'}, dimensions={0} | all-to-all | bytes 5767168 | tf_op jit(solution)/shard_map/all_to_all | solution.py:77
  102.3 0.4 convert_reduce_fusion.1
  102.7 0.2 fusion.59
  102.8 0.1 fusion.47
  103.0 0.3 fusion.73
  103.3 0.2 fusion.44
  103.6 0.1 copy.28
  103.7 0.3 broadcast_in_dim.78
  103.9 32.8 %all_to_all.36 = bf16[16,64,1024]{2,1,0:T(8,128)(2,1)S(1)} all-to-all(bf16[16,64,1024]{2,1,0:T(8,128)(2,1)S(1)} %broadcast_in_dim.78), channel_id=1, replica_groups=mesh['dp'=16,'section'=2,'tensor'=8] {'dp'}, dimensions={0} | all-to-all | bytes 4194304 | tf_op jit(solution)/shard_map/all_to_all | solution.py:53
  136.7 5.3 fusion.30
  142.0 0.0 all-gather.5.cloned.1.call-update
  142.0 0.0 all-gather.7.cloned.1.call-start
  142.1 172.8 %all-gather.5.cloned.1.call-done = bf16[8192,1024]{1,0:T(8,128)(2,1)} async-done(((bf16[1024,1024]{1,0:T(8,128)(2,1)}), bf16[8192,1024]{1,0:T(8,128)(2,1)}) %all-gather.5.cloned.1.call-update) | async-done | bytes 16777232 | tf_op jit(solution)/shard_map/all_gather | solution.py:94
  314.8 9.5 %reduce_sum.81 = bf16[1024,1024]{1,0:T(8,128)(2,1)S(1)} reduce(bf16[8,1024,1024]{2,1,0:T(8,128)(2,1)} %bitcast.107, bf16[]{:T(256)} %constant.80.clone.1), dimensions={0}, to_apply=%region_3.4 | reduce | flops 7340032 | bytes 18874370 | tf_op jit(solution)/shard_map/reduce_sum | solution.py:94
  324.3 0.0 copy-start.1
  324.3 0.0 copy-start.3
  324.3 2.5 fusion.3
  326.8 0.0 copy-done.1
  326.8 0.3 copy-done.3
  327.2 5.4 select_convert_fusion
  332.6 40.7 %all_to_all.37 = bf16[16,64,1408]{2,1,0:T(8,128)(2,1)S(1)} all-to-all(bf16[16,64,1408]{2,1,0:T(8,128)(2,1)S(1)} %bitcast.110), channel_id=1, replica_groups=mesh['dp'=16,'section'=2,'tensor'=8] {'dp'}, dimensions={0} | all-to-all | bytes 5767168 | tf_op jit(solution)/shard_map/all_to_all | solution.py:77
  373.3 0.4 convert_reduce_fusion
  373.7 0.2 fusion.55
  373.9 0.1 fusion.46
  374.0 0.3 fusion.74
  374.4 0.2 fusion.45
  374.6 0.1 copy.31
  374.7 0.3 broadcast_in_dim.82
  375.0 28.6 %all_to_all.38 = bf16[16,64,1024]{2,1,0:T(8,128)(2,1)S(1)} all-to-all(bf16[16,64,1024]{2,1,0:T(8,128)(2,1)S(1)} %broadcast_in_dim.82), channel_id=1, replica_groups=mesh['dp'=16,'section'=2,'tensor'=8] {'dp'}, dimensions={0} | all-to-all | bytes 4194304 | tf_op jit(solution)/shard_map/all_to_all | solution.py:53
  403.6 5.9 fusion.33
  409.5 0.0 all-gather.7.cloned.1.call-update
  409.5 168.6 %all-gather.7.cloned.1.call-done = bf16[8192,1024]{1,0:T(8,128)(2,1)} async-done(((bf16[1024,1024]{1,0:T(8,128)(2,1)}), bf16[8192,1024]{1,0:T(8,128)(2,1)}) %all-gather.7.cloned.1.call-update) | async-done | bytes 16777232 | tf_op jit(solution)/shard_map/all_gather | solution.py:94
  578.2 10.8 %reduce_sum.85 = bf16[1024,1024]{1,0:T(8,128)(2,1)} reduce(bf16[8,1024,1024]{2,1,0:T(8,128)(2,1)} %bitcast.108, bf16[]{:T(256)} %constant.80.clone.1), dimensions={0}, to_apply=%region_7.8 | reduce | flops 7340032 | bytes 18874370 | tf_op jit(solution)/shard_map/reduce_sum | solution.py:94
  588.9 5.0 fusion.5
  (17 shorter events, 0.2 us)
Async XLA Ops:
  9.8 7.7 %copy-start.4 = (bf16[1,1024,1,256]{3,1,2,0:T(8,128)(2,1)S(1)}, bf16[1,1024,1,256]{3,1,2,0:T(8,128)(2,1)}, u32[]{:S(2)}) copy-start(bf16[1,1024,1,256]{3,1,2,0:T(8,128)(2,1)} %param.12) | copy-start | bytes 1572868
  9.8 34.8 %all-to-all-start = ((bf16[64,16,1024]{2,0,1:T(8,128)(2,1)}), bf16[64,16,1024]{2,0,1:T(8,128)(2,1)}, u32[]{:S(2)}, u32[]{:S(2)}) async-start(bf16[64,16,1024]{2,0,1:T(8,128)(2,1)} %bitcast.104), calls=%async_computation | async-start | bytes 4194304 | tf_op jit(solution)/shard_map/all_to_all | solution.py:119
  17.4 27.2 %copy-start.6 = (f32[1,1024]{1,0:T(1,128)S(1)}, f32[1,1024]{1,0:T(1,128)}, u32[]{:S(2)}) copy-start(f32[1,1024]{1,0:T(1,128)} %param.10) | copy-start | bytes 12292
  17.4 28.6 %copy-start.5 = (s32[2048]{0:T(1024)S(1)}, s32[2048]{0:T(1024)}, u32[]{:S(2)}) copy-start(s32[2048]{0:T(1024)} %param.8) | copy-start | bytes 24580
  17.4 297.4 %all-gather.5.cloned.1.call-start = ((), (), s32[]{:S(2)}) async-start(), calls=%async_computation.5 | async-start | bytes 18874368 | tf_op jit(solution)/shard_map/all_gather | solution.py:94
  19.7 30.4 %collective-permute-start.1 = (bf16[1024,1408]{1,0:T(8,128)(2,1)S(1)}, bf16[1024,1408]{1,0:T(8,128)(2,1)}, u32[]{:S(2)}, u32[]{:S(2)}) collective-permute-start(bf16[1024,1408]{1,0:T(8,128)(2,1)S(1)} %maximum_maximum_fusion), channel_id=1, source_target_pairs={{0,8},{8,0},{1,9},{9,1},{2,10},{10,2},{3,11},{11,3},{4,12},{12,4},... | collective-permute-start | bytes 8650760 | tf_op jit(solution)/shard_map/ppermute | solution.py:115
  19.8 30.3 %collective-permute-start.2 = (bf16[1024,1024]{1,0:T(8,128)(2,1)}, bf16[1024,1024]{1,0:T(8,128)(2,1)}, u32[]{:S(2)}, u32[]{:S(2)}) collective-permute-start(bf16[1024,1024]{1,0:T(8,128)(2,1)} %bitcast.6), channel_id=1, source_target_pairs={{0,8},{8,0},{1,9},{9,1},{2,10},{10,2},{3,11},{11,3},{4,12},{12,4},... | collective-permute-start | bytes 6291464 | tf_op jit(solution)/shard_map/ppermute | solution.py:115
  44.6 5.5 collective-permute-start.3
  44.6 5.5 collective-permute-start
  50.1 4.9 copy-start.2
  55.0 3.6 copy-start
  142.0 436.1 %all-gather.7.cloned.1.call-start = ((), (), s32[]{:S(2)}) async-start(), calls=%async_computation.6 | async-start | bytes 18874368 | tf_op jit(solution)/shard_map/all_gather | solution.py:94
  324.3 2.5 copy-start.1
  324.3 2.8 copy-start.3
Sparse Core Ops, SparseCore 0:
  142.1 172.6 all-gather.4
  409.6 168.4 all-gather.6
